TPU v7x, 32 devices: a whole 2x2x4 slice. The times are simulated.
32 devices in a mesh: seq: 16 (over z, x, core), head: 2 (over y).
Axes of the slice: x: 2, y: 2, z: 4, core: 2. Of those that a mesh axis runs over, the one named last changes fastest.
Arguments:
- step_tokens: bfloat16 [2, 12, 8, 2560], P(None, None, None, 'head'), may hold values from -6 to 6
- parents: int32 [2, 12, 8], replicated, may hold values from 0 to 7
- tail_cache: bfloat16 [12, 8, 64, 2048], P(None, 'head', 'seq'), may hold values from -192 to 192
- tail_len: int32 [12], replicated, may hold values from 0 to 62, as said below
- cache: bfloat16 [8, 2048, 2048], P(None, ('seq', 'head')), may hold values from -192 to 192
- cache_len: int32 [8], replicated, may hold values from 256 to 2048, as said below
- prompt_states: bfloat16 [4, 128, 2560], P(None, 'seq', 'head'), may hold values from -6 to 6
- prompt_len: int32 [4], replicated, may hold values from 32 to 128, as said below
- in_gain: float32 [2560], P('head'), may hold values from 0.5 to 1.5
- w_query: bfloat16 [2560, 2048], P('head', 'seq'), may hold values from -0.125 to 0.125
- w_keyval: bfloat16 [2560, 2048], P('head', 'seq'), may hold values from -0.125 to 0.125
- q_gain: float32 [256], replicated, may hold values from 0.6 to 32
- k_gain: float32 [256], replicated, may hold values from 0.6 to 32
- w_out: bfloat16 [2048, 2560], P('seq', 'head'), may hold values from -0.125 to 0.125
- post_gain: float32 [2560], P('head'), may hold values from 0.5 to 1.5
- ffn_gain: float32 [2560], P('head'), may hold values from 0.5 to 1.5
- w_gate: bfloat16 [2560, 10240], P('head', 'seq'), may hold values from -0.125 to 0.125
- w_up: bfloat16 [2560, 10240], P('head', 'seq'), may hold values from -0.125 to 0.125
- w_down: bfloat16 [10240, 2560], P('seq', 'head'), may hold values from -0.0625 to 0.0625
- final_gain: float32 [2560], P('head'), may hold values from 0.5 to 1.5
Outputs:
- decoded: bfloat16 [2, 12, 8, 2560], P(None, None, None, 'head')
Inputs may be any that keep to these rules, and one draw needn't show every extreme that they name: `tail_len`: the first 4 groups have 0; the largest entry is exactly 62. `cache_len`: the largest entry is exactly 2048. `prompt_len`: the largest entry is exactly 128.
All inputs are finite; a program needn't handle non-finite values.
Results may differ from a plain program's by a relative error of at most 0.0055.
The roundings to bfloat16 on the way count: a program that leaves them out, or rounds other values in their place, can miss the bound.
Values may be sent and summed in bfloat16 or wider, within the bound.
No kernel may reach another device: no remote copies, remote signals or barrier semaphores. Data moves between devices by JAX's collectives and lax.ppermute only.
A program may use at most 128 MiB of HBM per device.

v0:
```python
import jax
import jax.numpy as jnp
from jax import lax
from jax.sharding import PartitionSpec as P

D = 2560
QH = 8
KVH = 4
HD = 256
QD = 2048
EPS = 1e-06
NEG = -1e30
QSCALE = 0.0625


def norm_heads(values, gain, scale):
    shaped = values.reshape(values.shape[:-1] + (-1, gain.shape[0]))
    shaped = shaped * lax.rsqrt(jnp.mean(shaped * shaped, -1, keepdims=True) + EPS) * gain * scale
    return shaped.reshape(values.shape)


def finish_keys(pairs, k_gain):
    half = pairs.shape[-1] // 2
    keys = norm_heads(pairs[..., :half], k_gain, 1.0)
    return jnp.concatenate([keys, pairs[..., half:]], -1).astype(jnp.bfloat16)


def split_pairs(pairs):
    half = pairs.shape[-1] // 2
    keys = pairs[..., :half].reshape(pairs.shape[:-1] + (KVH, HD))
    values = pairs[..., half:].reshape(pairs.shape[:-1] + (KVH, HD))
    return (keys, values)


def project_tokens(tokens, in_gain, w_query, w_keyval, q_gain, k_gain):
    flat = tokens.reshape(-1, tokens.shape[-1]).astype(jnp.float32)
    scaled = (flat * in_gain).astype(jnp.bfloat16)
    q_part = jnp.dot(scaled, w_query, preferred_element_type=jnp.float32)
    kv_part = jnp.dot(scaled, w_keyval, preferred_element_type=jnp.float32)
    squares = jnp.sum(flat * flat, -1)
    q_part, kv_part, squares = lax.psum((q_part, kv_part, squares), "head")
    factor = lax.rsqrt(squares / D + EPS)[:, None]
    q_raw = (q_part * factor).astype(jnp.bfloat16)
    kv_raw = (kv_part * factor).astype(jnp.bfloat16)
    block = q_raw.shape[1]
    both = lax.all_gather(jnp.concatenate([q_raw, kv_raw], 1), "seq", axis=1)
    q_raw = both[:, :, :block].reshape(both.shape[0], -1)
    kv_raw = both[:, :, block:].reshape(both.shape[0], -1)
    queries = norm_heads(q_raw.astype(jnp.float32), q_gain, QSCALE).astype(jnp.bfloat16)
    fresh = finish_keys(kv_raw.astype(jnp.float32), k_gain)
    return (queries, fresh)


def shards(
    step_tokens,
    parents,
    tail_cache,
    tail_len,
    cache,
    cache_len,
    prompt_states,
    prompt_len,
    in_gain,
    w_query,
    w_keyval,
    q_gain,
    k_gain,
    w_out,
    post_gain,
    ffn_gain,
    w_gate,
    w_up,
    w_down,
    final_gain,
):
    f32 = jnp.float32
    bf16 = jnp.bfloat16
    n_head = lax.axis_size("head")
    n_seq = lax.axis_size("seq")
    seq_at = lax.axis_index("seq")
    head_at = lax.axis_index("head")
    flat_at = seq_at * n_head + head_at
    steps, groups, beams, width = step_tokens.shape
    pre = prompt_states.shape[0]
    repeat = QH // KVH
    rows = jnp.transpose(prompt_states, (1, 0, 2)).astype(f32)
    prompt_scaled = (rows * in_gain).astype(bf16).reshape(-1, width)
    prompt_squares = jnp.sum(rows * rows, -1).reshape(-1)
    prompt_terms = jnp.dot(
        prompt_scaled,
        lax.all_gather(w_keyval, "seq", axis=1, tiled=True),
        preferred_element_type=f32,
    )
    prompt_sum, prompt_sq = (
        lax.psum_scatter(prompt_terms, "head", scatter_dimension=0, tiled=True),
        lax.psum_scatter(prompt_squares, "head", scatter_dimension=0, tiled=True),
    )
    prompt_pairs = finish_keys(prompt_sum * lax.rsqrt(prompt_sq / D + EPS)[:, None], k_gain)
    prompt_seg = prompt_pairs.shape[0] // pre
    prompt_pairs = jnp.transpose(prompt_pairs.reshape(prompt_seg, pre, -1), (1, 0, 2))
    prompt_keys, prompt_values = split_pairs(prompt_pairs)
    prompt_ok = (flat_at * prompt_seg + jnp.arange(prompt_seg))[None, :] < prompt_len[:, None]
    cache_seg = cache.shape[1]
    cache_keys, cache_values = split_pairs(cache)
    cache_ok = (flat_at * cache_seg + jnp.arange(cache_seg))[None, :] < cache_len[:, None]
    tail_seg = tail_cache.shape[2]
    local_beams = tail_cache.shape[1]
    offset = (seq_at * tail_seg + jnp.arange(tail_seg))[None, :] - tail_len[:, None]
    all_beams = jnp.arange(beams)
    every_query, every_fresh = project_tokens(
        step_tokens, in_gain, w_query, w_keyval, q_gain, k_gain
    )
    every_query = every_query.reshape(steps, groups, beams, -1)
    every_fresh = every_fresh.reshape(steps, groups, beams, -1)
    everyone = lax.all_gather(tail_cache, "head", axis=1, tiled=True)
    local_ids = head_at * local_beams + jnp.arange(local_beams)
    n_dev = n_seq * n_head
    owner = jnp.broadcast_to(all_beams[None, :, None], (groups, beams, tail_seg))
    source = jnp.broadcast_to(all_beams[None, :], (groups, beams))
    ancestors = []
    shaped_all, scores_all, tails_all = ([], [], [])
    for step in range(steps):
        link = parents[step]
        source = jnp.take_along_axis(source, link, axis=1)
        ancestors = [jnp.take_along_axis(a, link, axis=1) for a in ancestors]
        ancestors.append(jnp.broadcast_to(all_beams[None, :], (groups, beams)))
        picks = lax.dynamic_slice_in_dim(source, head_at * local_beams, local_beams, 1)
        tail_state = jnp.take_along_axis(everyone, picks[:, :, None, None], axis=1)
        for back, anc in enumerate(ancestors):
            mine = lax.dynamic_slice_in_dim(anc, head_at * local_beams, local_beams, 1)
            written = jnp.take_along_axis(every_fresh[back], mine[:, :, None], axis=1)
            tail_state = jnp.where(
                (offset == back)[:, None, :, None], written[:, :, None, :], tail_state
            )
        tail_ok = (offset <= step)[:, None, None, :] & (
            owner[:, :, None, :] == local_ids[None, None, :, None]
        )
        shaped = every_query[step].reshape(groups, beams, KVH, repeat, HD)
        tail_keys, tail_values = split_pairs(tail_state)
        pre_scores = jnp.einsum(
            "gbkrd,gtkd->gbkrt", shaped[:pre], prompt_keys, preferred_element_type=f32
        )
        dec_scores = jnp.einsum(
            "gbkrd,gtkd->gbkrt", shaped[pre:], cache_keys, preferred_element_type=f32
        )
        tail_scores = jnp.einsum(
            "gbkrd,gctkd->gbkrct", shaped, tail_keys, preferred_element_type=f32
        )
        pre_scores = jnp.where(prompt_ok[:, None, None, None, :], pre_scores, NEG)
        dec_scores = jnp.where(cache_ok[:, None, None, None, :], dec_scores, NEG)
        tail_scores = jnp.where(tail_ok[:, :, None, None, :, :], tail_scores, NEG)
        top = jnp.concatenate([jnp.max(pre_scores, -1), jnp.max(dec_scores, -1)], 0)
        top = jnp.maximum(top, jnp.max(tail_scores, (-2, -1)))
        scores_all.append((pre_scores, dec_scores, tail_scores))
        tails_all.append((tail_ok, tail_values))
        shaped_all.append(top)
    top_all = lax.pmax(jnp.stack(shaped_all), ("seq", "head"))
    weighted_all, total_all = ([], [])
    for step in range(steps):
        pre_scores, dec_scores, tail_scores = scores_all[step]
        tail_ok, tail_values = tails_all[step]
        top = top_all[step]
        pre_mask = prompt_ok[:, None, None, None, :]
        dec_mask = cache_ok[:, None, None, None, :]
        tail_mask = tail_ok[:, :, None, None, :, :]
        pre_weights = jnp.where(pre_mask, jnp.exp(pre_scores - top[:pre, ..., None]), 0.0)
        dec_weights = jnp.where(dec_mask, jnp.exp(dec_scores - top[pre:, ..., None]), 0.0)
        tail_weights = jnp.where(tail_mask, jnp.exp(tail_scores - top[..., None, None]), 0.0)
        total = jnp.concatenate([jnp.sum(pre_weights, -1), jnp.sum(dec_weights, -1)], 0)
        total = total + jnp.sum(tail_weights, (-2, -1))
        weighted = jnp.concatenate(
            [
                jnp.einsum(
                    "gbkrt,gtkd->gbkrd",
                    pre_weights.astype(bf16),
                    prompt_values,
                    preferred_element_type=f32,
                ),
                jnp.einsum(
                    "gbkrt,gtkd->gbkrd",
                    dec_weights.astype(bf16),
                    cache_values,
                    preferred_element_type=f32,
                ),
            ],
            0,
        )
        weighted = weighted + jnp.einsum(
            "gbkrct,gctkd->gbkrd",
            tail_weights.astype(bf16),
            tail_values,
            preferred_element_type=f32,
        )
        weighted_all.append(weighted.reshape(groups * beams, -1))
        total_all.append(total.reshape(groups * beams, -1))
    weighted = jnp.concatenate(weighted_all, 0)
    total = jnp.concatenate(total_all, 0)
    rows = weighted.shape[0]
    piece = QD // n_seq
    piece_head = jnp.arange(n_seq) * piece // HD
    lanes = -(-rows // 128) * 128
    packed = jnp.concatenate(
        [
            jnp.transpose(weighted.reshape(rows, n_seq, piece), (1, 0, 2)).reshape(n_seq, -1),
            jnp.pad(jnp.transpose(total[:, piece_head]), ((0, 0), (0, lanes - rows))),
        ],
        1,
    )
    packed = lax.psum_scatter(packed, "seq", scatter_dimension=0, tiled=True)
    packed = lax.psum(packed, "head")
    share = packed[0, : rows * piece].reshape(rows, piece)
    own_total = packed[0, rows * piece : rows * piece + rows]
    attn = (share / own_total[:, None]).astype(bf16)
    partial_out = jnp.dot(attn, w_out, preferred_element_type=f32)
    per_dev = rows // n_seq
    out_proj = lax.psum_scatter(
        partial_out.reshape(n_seq, per_dev, -1), "seq", scatter_dimension=0, tiled=True
    )[0]
    out_sq = lax.psum(jnp.sum(out_proj * out_proj, -1), "head")
    x_all = step_tokens.reshape(rows, -1)
    x_f = lax.dynamic_slice_in_dim(x_all, seq_at * per_dev, per_dev, 0).astype(f32)
    state = (x_f + out_proj * lax.rsqrt(out_sq / D + EPS)[:, None] * post_gain).astype(bf16)
    state_all = lax.all_gather(state, "seq", axis=0, tiled=True)
    state_f = state_all.astype(f32)
    scaled_two = (state_f * ffn_gain).astype(bf16)
    gate_part = jnp.dot(scaled_two, w_gate, preferred_element_type=f32)
    up_part = jnp.dot(scaled_two, w_up, preferred_element_type=f32)
    gate_part, up_part, state_sq = lax.psum(
        (gate_part, up_part, jnp.sum(state_f * state_f, -1)), "head"
    )
    norm_s = lax.rsqrt(state_sq / D + EPS)[:, None]
    inner = (jax.nn.gelu(gate_part * norm_s, approximate=True) * (up_part * norm_s)).astype(bf16)
    ffn_out = lax.psum_scatter(
        jnp.dot(inner, w_down, preferred_element_type=f32).reshape(n_seq, per_dev, -1),
        "seq",
        scatter_dimension=0,
        tiled=True,
    )[0]
    ffn_sq = lax.psum(jnp.sum(ffn_out * ffn_out, -1), "head")
    result = (
        state.astype(f32) + ffn_out * lax.rsqrt(ffn_sq / D + EPS)[:, None] * final_gain
    ).astype(bf16)
    result = lax.all_gather(result, "seq", axis=0, tiled=True)
    return result.reshape(steps, groups, beams, -1)


def solution(mesh):
    return jax.shard_map(
        shards,
        mesh=mesh,
        in_specs=(
            P(None, None, None, "head"),
            P(),
            P(None, "head", "seq", None),
            P(),
            P(None, ("seq", "head"), None),
            P(),
            P(None, "seq", "head"),
            P(),
            P("head"),
            P("head", "seq"),
            P("head", "seq"),
            P(),
            P(),
            P("seq", "head"),
            P("head"),
            P("head"),
            P("head", "seq"),
            P("head", "seq"),
            P("seq", "head"),
            P("head"),
        ),
        out_specs=P(None, None, None, "head"),
        check_vma=False,
    )
```

profile of v0, /device:TPU:0, one launch (start us, length us, event | category | flops | bytes accessed | tf_op | source)
XLA Modules:
  0.0 637.6 jit_solution(13518079163312761268)
XLA Ops:
  12.3 5.8 all-reduce.4
  18.1 18.1 %all-reduce.21.cloned.1.call-done = (f32[192,128]{1,0:T(8,128)}, f32[192,128]{1,0:T(8,128)}) async-done(((f32[192,128]{1,0:T(8,128)}, f32[192,128]{1,0:T(8,128)}), (f32[192,128]{1,0:T(8,128)}, f32[192,128]{1,0:T(8,128)})) %all-reduce.21.cloned.1.call-update) | async-done | bytes 196624 | tf_op jit(solution)/shard_map/psum | solution.py:41
  47.3 2.7 fusion.110
  50.0 2.6 reshape.490
  58.6 6.4 %all-gather.9.cloned.1.call-done = bf16[12,8,4,2048]{3,2,1,0:T(4,128)(2,1)} async-done(((bf16[12,4,4,2048]{3,2,1,0:T(4,128)(2,1)}), bf16[12,8,4,2048]{3,2,1,0:T(4,128)(2,1)}) %all-gather.9.cloned.1.call-update) | async-done | bytes 1572880 | tf_op jit(solution)/shard_map/all_gather | solution.py:115
  65.0 4.0 gather_fusion.8
  71.5 34.7 %all-gather.11.cloned.1.call-done = bf16[192,4096]{1,0:T(8,128)(2,1)} async-done(((bf16[192,256]{1,0:T(8,128)(2,1)}), bf16[192,4096]{1,0:T(8,128)(2,1)}) %all-gather.11.cloned.1.call-update) | async-done | bytes 1572880 | tf_op jit(solution)/shard_map/all_gather | solution.py:46
  135.0 3.0 fusion.38
  138.0 2.8 copy.257
  146.0 20.5 %all-gather.7.cloned.1.call-done = bf16[1280,2048]{1,0:T(8,128)(2,1)} async-done(((bf16[1280,128]{1,0:T(8,128)(2,1)}), bf16[1280,2048]{1,0:T(8,128)(2,1)}) %all-gather.7.cloned.1.call-update) | async-done | bytes 5242896 | tf_op jit(solution)/shard_map/all_gather | solution.py:91
  166.6 4.2 fusion.122
  174.6 6.2 reduce-scatter.4.cloned.1.call-done
  185.6 40.5 %pmax.7 = f32[2,12,8,4,2]{2,4,3,1,0:T(2,128)S(1)} all-reduce(f32[2,12,8,4,2]{2,4,3,1,0:T(2,128)S(1)} %pad_maximum_fusion.2), channel_id=1, replica_groups=mesh['seq'=16,'head'=2] {'seq','head'}, use_global_device_ids=true, to_apply=%region_17.21 | all-reduce | flops 1536 | bytes 12288 | tf_op jit(solution)/shard_map/pmax | solution.py:157
  254.6 94.9 %all-reduce.15.cloned.1.call-done = f32[16,24832]{1,0:T(8,128)} async-done(((f32[16,24832]{1,0:T(8,128)}), f32[16,24832]{1,0:T(8,128)}) %all-reduce.15.cloned.1.call-update) | async-done | bytes 1589264
  352.0 20.5 %all-reduce.13.cloned.1.call-done = f32[1,24832]{1,0:T(1,128)} async-done(((f32[1,24832]{1,0:T(1,128)}), f32[1,24832]{1,0:T(1,128)}) %all-reduce.13.cloned.1.call-update) | async-done | bytes 99344 | tf_op jit(solution)/shard_map/psum | solution.py:210
  375.9 94.0 %all-reduce.17.cloned.1.call-done = f32[16,12,1280]{2,0,1:T(8,128)} async-done(((f32[16,12,1280]{2,0,1:T(8,128)}), f32[16,12,1280]{2,0,1:T(8,128)}) %all-reduce.17.cloned.1.call-update) | async-done | bytes 983056
  471.7 4.9 psum.67
  477.5 21.2 %all-gather.1 = bf16[16,12,1280]{2,1,0:T(8,128)(2,1)S(1)} all-gather(bf16[1,12,1280]{2,1,0:T(8,128)(2,1)S(1)} %fusion.108), channel_id=1, replica_groups=mesh['seq'=16,'head'=2] {'seq'}, dimensions={0}, use_global_device_ids=true | all-gather | bytes 522240 | tf_op jit(solution)/shard_map/all_gather | solution.py:223
  498.8 2.9 fusion.55
  503.3 4.9 psum.69
  508.3 31.1 %all-reduce.19.cloned.1.call-done = (f32[192,640]{1,0:T(8,128)}, f32[192,640]{1,0:T(8,128)}) async-done(((f32[192,640]{1,0:T(8,128)}, f32[192,640]{1,0:T(8,128)}), (f32[192,640]{1,0:T(8,128)}, f32[192,640]{1,0:T(8,128)})) %all-reduce.19.cloned.1.call-update) | async-done | bytes 983056 | tf_op jit(solution)/shard_map/psum | solution.py:228
  542.5 59.1 %reduce-scatter.6.cloned.1.call-done = f32[1,12,1280]{2,1,0:T(8,128)} async-done(((f32[16,12,1280]{2,1,0:T(8,128)}), f32[1,12,1280]{2,1,0:T(8,128)}) %reduce-scatter.6.cloned.1.call-update) | async-done | bytes 61456 | tf_op jit(solution)/shard_map/reduce_scatter | solution.py:233
  602.6 4.9 psum.71
  608.6 21.3 %all-gather.2 = bf16[16,12,1280]{2,1,0:T(8,128)(2,1)S(1)} all-gather(bf16[1,12,1280]{2,1,0:T(8,128)(2,1)S(1)} %fusion.83), channel_id=1, replica_groups=mesh['seq'=16,'head'=2] {'seq'}, dimensions={0}, use_global_device_ids=true | all-gather | bytes 522240 | tf_op jit(solution)/shard_map/all_gather | solution.py:243
  (311 shorter events, 111.1 us)
Async XLA Ops:
  6.5 532.8 %copy-start = (bf16[640,1280]{1,0:T(8,128)(2,1)S(1)}, bf16[640,1280]{1,0:T(8,128)(2,1)}, u32[]{:S(2)}) copy-start(bf16[640,1280]{1,0:T(8,128)(2,1)} %param.44) | copy-start | bytes 4915204
  6.5 29.7 %all-reduce.21.cloned.1.call-start = ((), (), s32[]{:S(2)}) async-start(), calls=%async_computation.11 | async-start | bytes 393216 | tf_op jit(solution)/shard_map/psum | solution.py:41
  10.8 27.7 %copy-start.42 = (f32[256]{0:T(256)S(1)}, f32[256]{0:T(256)}, u32[]{:S(2)}) copy-start(f32[256]{0:T(256)} %param.38) | copy-start | bytes 3076
  10.8 27.8 %copy-start.45 = (s32[12]{0:T(128)S(1)}, s32[12]{0:T(128)}, u32[]{:S(2)}) copy-start(s32[12]{0:T(128)} %param.29) | copy-start | bytes 148
  10.9 28.6 %copy-start.43 = (f32[256]{0:T(256)S(1)}, f32[256]{0:T(256)}, u32[]{:S(2)}) copy-start(f32[256]{0:T(256)} %param.37) | copy-start | bytes 3076
  10.9 28.7 %copy-start.34 = (s32[2,12,8]{1,2,0:T(8,128)S(1)}, s32[2,12,8]{1,2,0:T(8,128)}, u32[]{:S(2)}) copy-start(s32[2,12,8]{1,2,0:T(8,128)} %param.27) | copy-start | bytes 2308
  10.9 54.1 %all-gather.9.cloned.1.call-start = ((), (), s32[]{:S(2)}) async-start(), calls=%async_computation.4 | async-start | bytes 2359296 | tf_op jit(solution)/shard_map/all_gather | solution.py:115
  11.6 94.5 %all-gather.11.cloned.1.call-start = ((), (), s32[]{:S(2)}) async-start(), calls=%async_computation.7 | async-start | bytes 1671168 | tf_op jit(solution)/shard_map/all_gather | solution.py:46
  37.9 128.7 %all-gather.7.cloned.1.call-start = ((), (), s32[]{:S(2)}) async-start(), calls=%async_computation.2 | async-start | bytes 5570560 | tf_op jit(solution)/shard_map/all_gather | solution.py:91
  38.5 142.3 %reduce-scatter.4.cloned.1.call-start = ((), (), s32[]{:S(2)}) async-start(), calls=%async_computation.3 | async-start | bytes 393216 | tf_op jit(solution)/shard_map/reduce_scatter | solution.py:95
  38.6 75.7 %copy-start.31 = (f32[1,2,4,128]{3,1,2,0:T(2,128)}, f32[1,2,4,128]{3,1,2,0:T(2,128)S(1)}, u32[]{:S(2)}) copy-start(f32[1,2,4,128]{3,1,2,0:T(2,128)S(1)} %copy.316) | copy-start | bytes 12292
  58.6 82.2 %copy-start.23 = (pred[12,8,4,4]{0,1,3,2:T(8,128)(4,1)}, pred[12,8,4,4]{0,1,3,2:T(8,128)(4,1)S(1)}, u32[]{:S(2)}) copy-start(pred[12,8,4,4]{0,1,3,2:T(8,128)(4,1)S(1)} %get-tuple-element.66) | copy-start | bytes 4612
  146.0 24.8 %copy-start.25 = (pred[12,8,4,4]{0,1,3,2:T(8,128)(4,1)S(1)}, pred[12,8,4,4]{0,1,3,2:T(8,128)(4,1)}, u32[]{:S(2)}) copy-start(pred[12,8,4,4]{0,1,3,2:T(8,128)(4,1)} %get-tuple-element.65) | copy-start | bytes 4612
  146.0 24.9 %copy-start.10 = (bf16[12,4,4,1024]{3,2,1,0:T(4,128)(2,1)S(1)}, bf16[12,4,4,1024]{3,2,1,0:T(4,128)(2,1)}, u32[]{:S(2)}) copy-start(bf16[12,4,4,1024]{3,2,1,0:T(4,128)(2,1)} %get-tuple-element.26) | copy-start | bytes 1179652
  170.8 178.7 %all-reduce.15.cloned.1.call-start = ((), (), s32[]{:S(2)}) async-start(), calls=%async_computation.8 | async-start | bytes 3178496
  182.1 48.6 %copy-start.14 = (f32[8,8,4,2,64]{4,1,3,2,0:T(8,128)S(1)}, f32[8,8,4,2,64]{4,1,3,2,0:T(8,128)}, u32[]{:S(2)}) copy-start(f32[8,8,4,2,64]{4,1,3,2,0:T(8,128)} %get-tuple-element.68) | copy-start | bytes 393220
  253.3 121.2 %copy-start.19 = (bf16[128,1280]{1,0:T(8,128)(2,1)S(1)}, bf16[128,1280]{1,0:T(8,128)(2,1)}, u32[]{:S(2)}) copy-start(bf16[128,1280]{1,0:T(8,128)(2,1)} %param.39) | copy-start | bytes 983044
  253.4 119.1 %all-reduce.13.cloned.1.call-start = ((), (), s32[]{:S(2)}) async-start(), calls=%async_computation.5 | async-start | bytes 198656 | tf_op jit(solution)/shard_map/psum | solution.py:210
  351.9 118.0 %all-reduce.17.cloned.1.call-start = ((), (), s32[]{:S(2)}) async-start(), calls=%async_computation.9 | async-start | bytes 1966080
  373.2 103.4 %copy-start.35 = (f32[1280]{0:T(1024)S(1)}, f32[1280]{0:T(1024)}, u32[]{:S(2)}) copy-start(f32[1280]{0:T(1024)} %param.40) | copy-start | bytes 15364
  375.8 123.0 %copy-start.33 = (f32[1280]{0:T(1024)S(1)}, f32[1280]{0:T(1024)}, u32[]{:S(2)}) copy-start(f32[1280]{0:T(1024)} %param.41) | copy-start | bytes 15364
  375.8 163.5 %all-reduce.19.cloned.1.call-start = ((), (), s32[]{:S(2)}) async-start(), calls=%async_computation.10 | async-start | bytes 1966080 | tf_op jit(solution)/shard_map/psum | solution.py:228
  503.1 98.5 %reduce-scatter.6.cloned.1.call-start = ((), (), s32[]{:S(2)}) async-start(), calls=%async_computation.6 | async-start | bytes 1392640 | tf_op jit(solution)/shard_map/reduce_scatter | solution.py:233
  541.3 66.3 %copy-start.40 = (f32[1280]{0:T(1024)S(1)}, f32[1280]{0:T(1024)}, u32[]{:S(2)}) copy-start(f32[1280]{0:T(1024)} %param.45) | copy-start | bytes 15364
  (36 other events, 203.8 us)
Sparse Core Ops, SparseCore 0:
  11.0 25.1 all-reduce.20
  37.7 27.1 all-gather.8
  67.2 38.9 all-gather.10
  108.2 58.3 all-gather.6
  170.9 9.8 reduce-scatter.3
  253.5 95.9 all-reduce.14
  352.0 20.3 all-reduce.12
  375.9 93.9 all-reduce.16
  503.2 36.0 all-reduce.18
  543.3 58.2 reduce-scatter.5
where the time goes:
time: 639 us; the launch traced here: 638 us
  waiting for transfers between devices  387 us (61%)
  blocking collectives  104 us (16%)
  local copies, waits for them, and re-layouts  66.5 us (10%)
  matrix products  35 us (5%)
  other arithmetic  30 us (5%)
  between operations  15.2 us (2%)
    unnamed x12, waiting for transfers between devices  190 us
    reduce_scatter x1, waiting for transfers between devices, shards(): lax.psum_scatter(jnp.dot(inner, w_down, preferred_element_type=f32).resha...  59.1 us
    pmax x1, blocking collectives, shards(): top_all = lax.pmax(jnp.stack(shaped_all), ('seq', 'head'))  40.5 us
    all_gather x1, waiting for transfers between devices, project_tokens(): both = lax.all_gather(jnp.concatenate([q_raw, kv_raw], 1), 'seq', axis=1)  34.7 us
    psum x1, waiting for transfers between devices, shards(): lax.psum((gate_part, up_part, jnp.sum(state_f * state_f, -1)), 'head')  31.1 us
    all_gather x1, blocking collectives, shards(): result = lax.all_gather(result, 'seq', axis=0, tiled=True)  21.3 us
    all_gather x1, blocking collectives, shards(): state_all = lax.all_gather(state, 'seq', axis=0, tiled=True)  21.2 us
    all_gather x1, waiting for transfers between devices, shards(): lax.all_gather(w_keyval, 'seq', axis=1, tiled=True)  20.5 us
  transfers between devices with their start and end apart: 10, of which 10 were waited for; matrix products, arithmetic and copies ran while one was open for 11% of the time, Pallas kernels for 0%

commit v1 on v0

--- a/solution.py
+++ b/solution.py
@@ -1,3 +1,4 @@
+import functools
 import jax
 import jax.numpy as jnp
 from jax import lax
@@ -11,6 +12,23 @@
 EPS = 1e-06
 NEG = -1e30
 QSCALE = 0.0625
+
+
+def check_state(tile_in, mesh_name, out_dim):
+    cores_n = jax.lax.axis_size(mesh_name)
+    tile_out = sorted(((no, (no + 1) % cores_n) for no in range(cores_n)))
+    x_new = tile_in
+    all_rows = [x_new]
+    for dev_j in range(1, cores_n):
+        x_new = jax.lax.ppermute(x_new, mesh_name, tile_out)
+        all_rows.insert(0, x_new)
+    response = jnp.concatenate(all_rows, axis=out_dim)
+    side_arr = jax.lax.axis_index(mesh_name) + 1
+    before = jnp.roll(response, side_arr * tile_in.shape[out_dim], axis=out_dim)
+    return before
+
+
+resolve_the_widths = functools.partial(check_state, mesh_name="seq", out_dim=0)
 
 
 def norm_heads(values, gain, scale):
@@ -220,7 +238,7 @@
     x_all = step_tokens.reshape(rows, -1)
     x_f = lax.dynamic_slice_in_dim(x_all, seq_at * per_dev, per_dev, 0).astype(f32)
     state = (x_f + out_proj * lax.rsqrt(out_sq / D + EPS)[:, None] * post_gain).astype(bf16)
-    state_all = lax.all_gather(state, "seq", axis=0, tiled=True)
+    state_all = resolve_the_widths(state)
     state_f = state_all.astype(f32)
     scaled_two = (state_f * ffn_gain).astype(bf16)
     gate_part = jnp.dot(scaled_two, w_gate, preferred_element_type=f32)

time: 639 us -> 722 us (1.13); the launches traced: 638 us -> 712 us
  waiting for transfers between devices: 387 us -> 478 us
  blocking collectives: 104 us -> 82.4 us
    ppermute x0 -> x15, waiting for transfers between devices: none -> 91.8 us  [check_state(): x_new = jax.lax.ppermute(x_new, mesh_name, tile_out)]
    all_gather x1 -> x0, blocking collectives: 21.2 us -> none  [shards(): state_all = lax.all_gather(state, 'seq', axis=0, tiled=True)]
  transfers between devices with their start and end apart: 10 -> 25, of which waited for: 10 -> 25; matrix products, arithmetic and copies ran while one was open for 11% -> 10% of each run, Pallas kernels for 0% -> 0%
where the time goes in v1:
time: 722 us; the launch traced here: 712 us
  waiting for transfers between devices  478 us (66%)
  blocking collectives  82.4 us (11%)
  local copies, waits for them, and re-layouts  70 us (10%)
  matrix products  35.1 us (5%)
  other arithmetic  30.5 us (4%)
  between operations  15.5 us (2%)
    unnamed x12, waiting for transfers between devices  190 us
    ppermute x15, waiting for transfers between devices, check_state(): x_new = jax.lax.ppermute(x_new, mesh_name, tile_out)  91.8 us
    reduce_scatter x1, waiting for transfers between devices, shards(): lax.psum_scatter(jnp.dot(inner, w_down, preferred_element_type=f32).resha...  59.1 us
    pmax x1, blocking collectives, shards(): top_all = lax.pmax(jnp.stack(shaped_all), ('seq', 'head'))  40.4 us
    all_gather x1, waiting for transfers between devices, project_tokens(): both = lax.all_gather(jnp.concatenate([q_raw, kv_raw], 1), 'seq', axis=1)  34.7 us
    psum x1, waiting for transfers between devices, shards(): lax.psum((gate_part, up_part, jnp.sum(state_f * state_f, -1)), 'head')  30.9 us
    all_gather x1, blocking collectives, shards(): result = lax.all_gather(result, 'seq', axis=0, tiled=True)  21.3 us
    psum x1, waiting for transfers between devices, shards(): packed = lax.psum(packed, 'head')  20.5 us
  transfers between devices with their start and end apart: 25, of which 25 were waited for; matrix products, arithmetic and copies ran while one was open for 10% of the time, Pallas kernels for 0%

profile of v1, /device:TPU:0, one launch (start us, length us, event | category | flops | bytes accessed | tf_op | source)
XLA Modules:
  0.0 711.8 jit_solution(14731672712614422369)
XLA Ops:
  18.1 18.1 %all-reduce.21.cloned.1.call-done = (f32[192,128]{1,0:T(8,128)}, f32[192,128]{1,0:T(8,128)}) async-done(((f32[192,128]{1,0:T(8,128)}, f32[192,128]{1,0:T(8,128)}), (f32[192,128]{1,0:T(8,128)}, f32[192,128]{1,0:T(8,128)})) %all-reduce.21.cloned.1.call-update) | async-done | bytes 196624 | tf_op jit(solution)/shard_map/psum | solution.py:59
  71.5 34.7 %all-gather.10.cloned.1.call-done = bf16[192,4096]{1,0:T(8,128)(2,1)} async-done(((bf16[192,256]{1,0:T(8,128)(2,1)}), bf16[192,4096]{1,0:T(8,128)(2,1)}) %all-gather.10.cloned.1.call-update) | async-done | bytes 1572880 | tf_op jit(solution)/shard_map/all_gather | solution.py:64
  146.3 20.3 %all-gather.6.cloned.1.call-done = bf16[1280,2048]{1,0:T(8,128)(2,1)} async-done(((bf16[1280,128]{1,0:T(8,128)(2,1)}), bf16[1280,2048]{1,0:T(8,128)(2,1)}) %all-gather.6.cloned.1.call-update) | async-done | bytes 5242896 | tf_op jit(solution)/shard_map/all_gather | solution.py:109
  174.7 6.2 reduce-scatter.4.cloned.1.call-done
  185.6 40.4 %pmax.7 = f32[2,12,8,4,2]{2,4,3,1,0:T(2,128)S(1)} all-reduce(f32[2,12,8,4,2]{2,4,3,1,0:T(2,128)S(1)} %pad_maximum_fusion.2), channel_id=1, replica_groups=mesh['seq'=16,'head'=2] {'seq','head'}, use_global_device_ids=true, to_apply=%region_17.21 | all-reduce | flops 1536 | bytes 12288 | tf_op jit(solution)/shard_map/pmax | solution.py:175
  254.7 94.8 %all-reduce.15.cloned.1.call-done = f32[16,24832]{1,0:T(8,128)} async-done(((f32[16,24832]{1,0:T(8,128)}), f32[16,24832]{1,0:T(8,128)}) %all-reduce.15.cloned.1.call-update) | async-done | bytes 1589264
  352.1 20.5 %all-reduce.13.cloned.1.call-done = f32[1,24832]{1,0:T(1,128)} async-done(((f32[1,24832]{1,0:T(1,128)}), f32[1,24832]{1,0:T(1,128)}) %all-reduce.13.cloned.1.call-update) | async-done | bytes 99344 | tf_op jit(solution)/shard_map/psum | solution.py:228
  376.0 94.0 %all-reduce.17.cloned.1.call-done = f32[16,12,1280]{2,0,1:T(8,128)} async-done(((f32[16,12,1280]{2,0,1:T(8,128)}), f32[16,12,1280]{2,0,1:T(8,128)}) %all-reduce.17.cloned.1.call-update) | async-done | bytes 983056
  483.9 6.1 collective-permute-done.1
  490.1 6.1 collective-permute-done.2
  496.2 6.1 collective-permute-done.3
  502.3 6.1 collective-permute-done.4
  508.4 6.1 collective-permute-done.5
  514.6 6.1 collective-permute-done.6
  520.7 6.1 collective-permute-done.7
  526.8 6.1 collective-permute-done.8
  532.9 6.1 collective-permute-done.9
  539.0 6.1 collective-permute-done.10
  545.2 6.1 collective-permute-done.11
  551.3 6.1 collective-permute-done.12
  557.4 6.1 collective-permute-done.13
  582.4 30.9 %all-reduce.19.cloned.1.call-done = (f32[192,640]{1,0:T(8,128)}, f32[192,640]{1,0:T(8,128)}) async-done(((f32[192,640]{1,0:T(8,128)}, f32[192,640]{1,0:T(8,128)}), (f32[192,640]{1,0:T(8,128)}, f32[192,640]{1,0:T(8,128)})) %all-reduce.19.cloned.1.call-update) | async-done | bytes 983056 | tf_op jit(solution)/shard_map/psum | solution.py:246
  616.5 59.1 %reduce-scatter.6.cloned.1.call-done = f32[1,12,1280]{2,1,0:T(8,128)} async-done(((f32[16,12,1280]{2,1,0:T(8,128)}), f32[1,12,1280]{2,1,0:T(8,128)}) %reduce-scatter.6.cloned.1.call-update) | async-done | bytes 61456 | tf_op jit(solution)/shard_map/reduce_scatter | solution.py:251
  682.6 21.3 %all-gather.1 = bf16[16,12,1280]{2,1,0:T(8,128)(2,1)S(1)} all-gather(bf16[1,12,1280]{2,1,0:T(8,128)(2,1)S(1)} %fusion.87), channel_id=1, replica_groups=mesh['seq'=16,'head'=2] {'seq'}, dimensions={0}, use_global_device_ids=true | all-gather | bytes 522240 | tf_op jit(solution)/shard_map/all_gather | solution.py:261
  (340 shorter events, 176.4 us)
Async XLA Ops:
  6.5 29.7 %all-reduce.21.cloned.1.call-start = ((), (), s32[]{:S(2)}) async-start(), calls=%async_computation.11 | async-start | bytes 393216 | tf_op jit(solution)/shard_map/psum | solution.py:59
  10.9 54.1 %all-gather.8.cloned.1.call-start = ((), (), s32[]{:S(2)}) async-start(), calls=%async_computation.4 | async-start | bytes 2359296 | tf_op jit(solution)/shard_map/all_gather | solution.py:133
  11.6 94.5 %all-gather.10.cloned.1.call-start = ((), (), s32[]{:S(2)}) async-start(), calls=%async_computation.7 | async-start | bytes 1671168 | tf_op jit(solution)/shard_map/all_gather | solution.py:64
  37.9 128.6 %all-gather.6.cloned.1.call-start = ((), (), s32[]{:S(2)}) async-start(), calls=%async_computation.2 | async-start | bytes 5570560 | tf_op jit(solution)/shard_map/all_gather | solution.py:109
  38.5 142.3 %reduce-scatter.4.cloned.1.call-start = ((), (), s32[]{:S(2)}) async-start(), calls=%async_computation.3 | async-start | bytes 393216 | tf_op jit(solution)/shard_map/reduce_scatter | solution.py:113
  170.8 178.7 %all-reduce.15.cloned.1.call-start = ((), (), s32[]{:S(2)}) async-start(), calls=%async_computation.8 | async-start | bytes 3178496
  253.4 119.2 %all-reduce.13.cloned.1.call-start = ((), (), s32[]{:S(2)}) async-start(), calls=%async_computation.5 | async-start | bytes 198656 | tf_op jit(solution)/shard_map/psum | solution.py:228
  352.1 117.9 %all-reduce.17.cloned.1.call-start = ((), (), s32[]{:S(2)}) async-start(), calls=%async_computation.9 | async-start | bytes 1966080
  375.9 237.5 %all-reduce.19.cloned.1.call-start = ((), (), s32[]{:S(2)}) async-start(), calls=%async_computation.10 | async-start | bytes 1966080 | tf_op jit(solution)/shard_map/psum | solution.py:246
  477.7 6.2 collective-permute-start
  483.9 6.1 collective-permute-start.1
  490.0 6.1 collective-permute-start.2
  496.2 6.1 collective-permute-start.3
  502.3 6.1 collective-permute-start.4
  508.4 6.1 collective-permute-start.5
  514.5 6.1 collective-permute-start.6
  520.7 6.1 collective-permute-start.7
  526.8 6.1 collective-permute-start.8
  532.9 6.1 collective-permute-start.9
  539.0 6.1 collective-permute-start.10
  545.2 6.1 collective-permute-start.11
  551.3 6.1 collective-permute-start.12
  557.4 6.1 collective-permute-start.13
  577.2 98.5 %reduce-scatter.6.cloned.1.call-start = ((), (), s32[]{:S(2)}) async-start(), calls=%async_computation.6 | async-start | bytes 1392640 | tf_op jit(solution)/shard_map/reduce_scatter | solution.py:251
  (51 other events, 1673.7 us)
Sparse Core Ops, SparseCore 0:
  11.0 25.1 all-reduce.20
  37.7 27.2 all-gather.7
  67.2 38.9 all-gather.9
  108.2 58.3 all-gather.5
  170.9 9.8 reduce-scatter.3
  253.5 95.9 all-reduce.14
  352.2 20.3 all-reduce.12
  376.0 93.9 all-reduce.16
  577.3 36.0 all-reduce.18
  617.3 58.2 reduce-scatter.5
